TPU v7x, 32 devices: a whole 2x2x4 slice. The times are simulated.
32 devices in a mesh: group: 2 (over y), seq: 4 (over z), batch: 2 (over x), chan: 2 (over core).
Axes of the slice: x: 2, y: 2, z: 4, core: 2. Of those that a mesh axis runs over, the one named last changes fastest.
Arguments:
- seq_in: bfloat16 [4, 4096, 768], P(('group', 'batch'), 'seq', 'chan'), parts along dimension 0, may hold values from -6 to 6
- conv_weight: bfloat16 [3, 768, 768], P(None, 'chan'), may hold values from -0.125 to 0.125
- cotangent: bfloat16 [4, 2048, 768], P(('group', 'batch'), 'seq', 'chan'), parts along dimension 0, may hold values from -0.59765625 to 0.59765625
Outputs:
- block_out: bfloat16 [4, 2048, 768], P(('group', 'batch'), 'seq', 'chan'), parts along dimension 0
- input_grad: bfloat16 [4, 4096, 768], P(('group', 'batch'), 'seq', 'chan'), parts along dimension 0
- weight_grad: float32 [6, 768, 768], P('group', 'chan', 'batch'), parts along dimension 0
There are 2 independent parts, one for each index of `group`. A program takes and returns all parts, laid end to end along the dimension named above; an argument that names none is the same for every part. Nothing has to cross between parts.
All inputs are finite; a program needn't handle non-finite values.
Results may differ from a plain program's by a relative error of at most 0.0031.
Values may be sent and summed in bfloat16 or wider, within the bound.
No kernel may reach another device: no remote copies, remote signals or barrier semaphores. Data moves between devices by JAX's collectives and lax.ppermute only.
A program may use at most 64 MiB of HBM per device.

v0:
```python
import jax
import jax.numpy as jnp
from jax import lax
from jax.sharding import PartitionSpec as P


def shift_from(block, axis, distance):
    size = lax.axis_size(axis)
    route = [(i - distance, i) for i in range(size) if 0 <= i - distance < size]
    return lax.ppermute(block, axis, route)


def half_of(array, index, axis):
    parts = 2
    shape = array.shape
    split = shape[:axis] + (parts, shape[axis] // parts) + shape[axis + 1 :]
    return lax.dynamic_index_in_dim(array.reshape(split), index, axis, keepdims=False)


def shards(seq_in, conv_weight, cotangent):
    local_in = seq_in[0]
    local_cot = cotangent[0]
    rows = local_in.shape[0] // 2
    width = local_in.shape[1]
    spread = rows // 2
    pooled = 0.5 * jnp.sum(local_in.astype(jnp.float32).reshape(rows, 2, width), axis=1)
    activation = jax.nn.gelu(pooled).astype(jnp.bfloat16)
    both = jnp.stack([activation, local_cot])
    from_prev = shift_from(both[:, rows - spread :], "seq", 1)
    from_next = shift_from(both[:, :spread], "seq", -1)
    own_ext = jnp.concatenate([from_prev, both, from_next], 1)
    full_ext = lax.all_gather(own_ext, "chan", axis=2, tiled=True)
    act_full, cot_full = (full_ext[0], full_ext[1])
    weight_cols = lax.all_to_all(conv_weight, "chan", 2, 1, tiled=True)
    act_taps = jnp.stack([act_full[k * spread : k * spread + rows] for k in range(3)], 1)
    conv_out = jnp.dot(
        act_taps.reshape(rows, -1),
        weight_cols.reshape(-1, weight_cols.shape[2]),
        preferred_element_type=jnp.float32,
    )
    block_out = (pooled + conv_out).astype(jnp.bfloat16)
    cot_taps = jnp.stack(
        [cot_full[(2 - k) * spread : (2 - k) * spread + rows] for k in range(3)], 1
    )
    activ_grad = jnp.einsum(
        "tko,kio->ti", cot_taps, conv_weight, preferred_element_type=jnp.float32
    )
    unused, gelu_back = jax.vjp(jax.nn.gelu, pooled)
    pooled_grad = local_cot.astype(jnp.float32) + gelu_back(activ_grad)[0]
    input_grad = jnp.repeat(0.5 * pooled_grad, 2, axis=0).astype(jnp.bfloat16)
    own_taps = jnp.stack([own_ext[0, k * spread : k * spread + rows] for k in range(3)], 1)
    cot_mid = cot_full[spread : spread + rows]
    batch_count = lax.axis_size("batch")
    if batch_count == 2:
        b = lax.axis_index("batch")
        send = jnp.einsum(
            "tki,to->kio", own_taps, half_of(cot_mid, 1 - b, 1), preferred_element_type=jnp.float32
        )
        keep = jnp.einsum(
            "tki,to->kio", own_taps, half_of(cot_mid, b, 1), preferred_element_type=jnp.float32
        )
        summed = keep + lax.ppermute(send, "batch", [(0, 1), (1, 0)])
    else:
        partial = jnp.einsum("tki,to->kio", own_taps, cot_mid, preferred_element_type=jnp.float32)
        summed = lax.psum_scatter(partial, "batch", scatter_dimension=2, tiled=True)
    weight_grad = lax.psum(summed, "seq")
    return (block_out[None], input_grad[None], weight_grad)


def solution(mesh):
    in_specs = (
        P(("group", "batch"), "seq", "chan"),
        P(None, "chan", None),
        P(("group", "batch"), "seq", "chan"),
    )
    out_specs = (
        P(("group", "batch"), "seq", "chan"),
        P(("group", "batch"), "seq", "chan"),
        P("group", "chan", "batch"),
    )
    return jax.shard_map(shards, mesh=mesh, in_specs=in_specs, out_specs=out_specs, check_vma=False)
```

profile of v0, /device:TPU:0, one launch (start us, length us, event | category | flops | bytes accessed | tf_op | source)
XLA Modules:
  0.0 179.5 jit_solution(5351627847527597983)
XLA Ops:
  7.2 0.0 all-gather.2.cloned.1.call-start
  7.2 2.2 %reshape.129 = f32[512,2,384]{2,1,0:T(2,128)S(1)} reshape(bf16[1,1024,384]{2,1,0:T(8,128)(2,1)} %param.3) | data formatting | bytes 2359296 | tf_op jit(solution)/shard_map/convert_element_type | solution.py:26
  9.4 0.0 copy-start
  9.4 1.9 %reduce_sum.9 = f32[512,384]{1,0:T(8,128)S(1)} reduce(f32[512,2,384]{2,1,0:T(2,128)S(1)} %reshape.129, f32[]{:T(128)} %constant.8.clone.1), dimensions={1}, to_apply=%region_0.0 | reduce | flops 196608 | bytes 2359300 | tf_op jit(solution)/shard_map/reduce_sum | solution.py:26
  11.3 0.3 fusion.27
  11.6 0.0 copy-done
  11.6 0.1 fusion.39
  11.7 5.0 %collective-permute-start = (bf16[2,256,384]{2,1,0:T(8,128)(2,1)S(1)}, bf16[2,256,384]{2,1,0:T(8,128)(2,1)S(1)}, u32[]{:S(2)}, u32[]{:S(2)}) collective-permute-start(bf16[2,256,384]{2,1,0:T(8,128)(2,1)S(1)} %get-tuple-element.14), channel_id=1, source_target_pairs={{0,4},{4,8},{8,12},{1,5},{5,9},{9,13},{2,6},{6,10},{10,14},{3,7},{... | collective-permute-start | bytes 1179656 | tf_op jit(solution)/shard_map/ppermute | solution.py:10
  16.7 1.3 collective-permute-start.1
  18.0 7.0 %collective-permute-done = bf16[2,256,384]{2,1,0:T(8,128)(2,1)S(1)} collective-permute-done((bf16[2,256,384]{2,1,0:T(8,128)(2,1)S(1)}, bf16[2,256,384]{2,1,0:T(8,128)(2,1)S(1)}, u32[]{:S(2)}, u32[]{:S(2)}) %collective-permute-start) | collective-permute-done | bytes 393248 | tf_op jit(solution)/shard_map/ppermute | solution.py:10
  25.0 4.1 %collective-permute-done.1 = bf16[2,256,384]{2,1,0:T(8,128)(2,1)S(1)} collective-permute-done((bf16[2,256,384]{2,1,0:T(8,128)(2,1)S(1)}, bf16[2,256,384]{2,1,0:T(8,128)(2,1)S(1)}, u32[]{:S(2)}, u32[]{:S(2)}) %collective-permute-start.1) | collective-permute-done | bytes 393248 | tf_op jit(solution)/shard_map/ppermute | solution.py:10
  29.1 1.3 pad_maximum_fusion.1
  30.4 0.0 all-gather.2.cloned.1.call-update
  30.5 0.0 all-reduce.2.cloned.1.call-start
  30.5 1.0 fusion.35
  31.6 0.1 fusion.41
  31.6 11.2 %all-gather.2.cloned.1.call-done = bf16[2,1024,768]{2,1,0:T(8,128)(2,1)} async-done(((bf16[2,1024,384]{2,1,0:T(8,128)(2,1)}), bf16[2,1024,768]{2,1,0:T(8,128)(2,1)}) %all-gather.2.cloned.1.call-update) | async-done | bytes 3145744 | tf_op jit(solution)/shard_map/all_gather | solution.py:32
  42.8 4.6 %fusion.45 = (bf16[1,512,768]{2,1,0:T(8,128)(2,1)S(1)}, bf16[512,1,768]{2,0,1:T(8,128)(2,1)}, bf16[512,1,768]{2,0,1:T(8,128)(2,1)}, bf16[512,1,768]{2,0,1:T(8,12...) fusion(bf16[2,1024,768]{2,1,0:T(8,128)(2,1)} %all-gather.2.cloned.1.call-done), kind=kLoop, calls=%fused_computation.67 | loop fusion | bytes 10223616 | tf_op jit(solution)/shard_map/slice | solution.py:43
  47.4 0.2 reshape.128
  47.6 0.0 copy-start.1
  47.6 1.6 constant_dynamic-slice_fusion.1
  49.3 0.0 copy-done.1
  49.3 0.8 fusion.38
  50.1 1.8 %collective-permute-start.2 = (f32[3,384,384]{2,1,0:T(8,128)S(1)}, f32[3,384,384]{2,1,0:T(8,128)S(1)}, u32[]{:S(2)}, u32[]{:S(2)}) collective-permute-start(f32[3,384,384]{2,1,0:T(8,128)S(1)} %fusion.38), channel_id=1, source_target_pairs={{0,2},{2,0},{1,3},{3,1},{4,6},{6,4},{5,7},{7,5},{8,10},{10,8},{9,1... | collective-permute-start | bytes 5308424 | tf_op jit(solution)/shard_map/ppermute | solution.py:62
  51.9 39.1 %collective-permute-done.2 = f32[3,384,384]{2,1,0:T(8,128)S(1)} collective-permute-done((f32[3,384,384]{2,1,0:T(8,128)S(1)}, f32[3,384,384]{2,1,0:T(8,128)S(1)}, u32[]{:S(2)}, u32[]{:S(2)}) %collective-permute-start.2) | collective-permute-done | bytes 1769504 | tf_op jit(solution)/shard_map/ppermute | solution.py:62
  91.0 2.0 %convolution_add_fusion = f32[3,384,384]{2,1,0:T(8,128)} fusion(f32[3,384,384]{2,1,0:T(8,128)S(1)} %collective-permute-done.2, bf16[512,1,384]{2,0,1:T(8,128)(2,1)S(1)} %get-tuple-element.13, bf16[512,1,384]{2,0,1:T(8,128)(2,1)S(1)} %copy-done.1, bf16[512,1,384]{2,0,1:T(8,128)(2,1)S(1)} %get-tuple-element.12, bf16[512,1,384]{2,1,0:T(2,128)(2,1)S(1)} %get-tuple-element.10), kind=kOutput, calls=%fused_computation.8 | convolution fusion | flops 454606848 | bytes 5111808 | tf_op jit(solution)/shard_map/tki,to->kio/dot_general | solution.py:59
  93.0 0.0 all-reduce.2.cloned.1.call-update
  93.0 4.0 %copy.21 = bf16[3,384,768]{1,0,2:T(4,128)(2,1)S(1)} copy(bf16[3,384,768]{2,1,0:T(8,128)(2,1)} %param.4) | data formatting | bytes 3538944 | tf_op args[1]
  97.0 5.6 %all_to_all.15 = bf16[3,384,768]{1,0,2:T(4,128)(2,1)S(1)} all-to-all(bf16[3,384,768]{1,0,2:T(4,128)(2,1)S(1)} %copy.21), channel_id=1, replica_groups=mesh['group'=2,'seq'=4,'batch'=2,'chan'=2] {'chan'}, dimensions={2} | all-to-all | bytes 3538944 | tf_op jit(solution)/shard_map/all_to_all | solution.py:34
  102.6 0.2 copy.22
  102.9 2.3 %copy.23 = bf16[3,2,384,384]{3,2,1,0:T(8,128)(2,1)} copy(bf16[3,2,384,384]{2,3,1,0:T(8,128)(2,1)S(1)} %bitcast.46) | data formatting | bytes 3538944 | tf_op jit(solution)/shard_map/all_to_all | solution.py:34
  105.1 4.0 %fusion.19 = bf16[512,384]{1,0:T(8,128)(2,1)S(1)} fusion(bf16[3,384,768]{2,1,0:T(8,128)(2,1)} %param.4, bf16[512,1,768]{2,0,1:T(8,128)(2,1)} %get-tuple-element.5, bf16[512,1,768]{2,0,1:T(8,128)(2,1)} %get-tuple-element.4, bf16[512,1,768]{2,0,1:T(8,128)(2,1)} %get-tuple-element.6, f32[512,384]{1,0:T(8,128)S(1)} %reduce_sum.9, ...), kind=kOutput, calls=%fused_computation.26 | convolution fusion | flops 913047552 | bytes 5701632 | tf_op jit(solution)/shard_map/tko,kio->ti/dot_general | solution.py:45
  109.2 0.4 broadcast_in_dim.8
  109.6 1.2 convert_element_type.60
  110.8 1.9 %pad_maximum_fusion = bf16[512,3,768]{2,0,1:T(8,128)(2,1)S(1)} fusion(bf16[512,1,768]{2,0,1:T(8,128)(2,1)} %get-tuple-element.7, bf16[512,1,768]{2,0,1:T(8,128)(2,1)} %get-tuple-element.8, bf16[512,1,768]{2,0,1:T(8,128)(2,1)} %get-tuple-element.9), kind=kLoop, calls=%fused_computation | loop fusion | flops 2359296 | bytes 4718592 | tf_op jit(solution)/shard_map/stack | solution.py:35
  112.7 2.5 %copy.20 = bf16[512,3,768]{0,2,1:T(8,128)(2,1)} copy(bf16[512,3,768]{2,0,1:T(8,128)(2,1)S(1)} %pad_maximum_fusion) | data formatting | bytes 4718592 | tf_op jit(solution)/shard_map/stack | solution.py:35
  115.2 4.4 %fusion.10 = bf16[1,512,384]{2,1,0:T(8,128)(2,1)} fusion(bf16[512,2304]{0,1:T(8,128)(2,1)} %bitcast.45, bf16[2304,384]{1,0:T(8,128)(2,1)} %bitcast.47, f32[512,384]{1,0:T(8,128)S(1)} %reduce_sum.9), kind=kOutput, calls=%fused_computation.12 | convolution fusion | flops 906559488 | bytes 5308416 | tf_op jit(solution)/shard_map/dot_general | solution.py:36
  119.6 50.3 %all-reduce.2.cloned.1.call-done = f32[3,384,384]{2,1,0:T(8,128)} async-done(((f32[3,384,384]{2,1,0:T(8,128)}), f32[3,384,384]{2,1,0:T(8,128)}) %all-reduce.2.cloned.1.call-update) | async-done | bytes 1769488 | tf_op jit(solution)/shard_map/psum | solution.py:66
  169.8 2.8 %copy.37 = f32[3,384,384]{2,1,0:T(8,128)} copy(f32[3,384,384]{2,1,0:T(8,128)} %all-reduce.2.cloned.1.call-done) | data formatting | bytes 3538944
Async XLA Ops:
  7.2 35.7 %all-gather.2.cloned.1.call-start = ((), (), s32[]{:S(2)}) async-start(), calls=%async_computation.1 | async-start | bytes 4718592 | tf_op jit(solution)/shard_map/all_gather | solution.py:32
  9.4 2.2 %copy-start = (bf16[1,512,384]{2,1,0:T(8,128)(2,1)S(1)}, bf16[1,512,384]{2,1,0:T(8,128)(2,1)}, u32[]{:S(2)}) copy-start(bf16[1,512,384]{2,1,0:T(8,128)(2,1)} %param.5) | copy-start | bytes 1179652
  11.7 13.3 %collective-permute-start = (bf16[2,256,384]{2,1,0:T(8,128)(2,1)S(1)}, bf16[2,256,384]{2,1,0:T(8,128)(2,1)S(1)}, u32[]{:S(2)}, u32[]{:S(2)}) collective-permute-start(bf16[2,256,384]{2,1,0:T(8,128)(2,1)S(1)} %get-tuple-element.14), channel_id=1, source_target_pairs={{0,4},{4,8},{8,12},{1,5},{5,9},{9,13},{2,6},{6,10},{10,14},{3,7},{... | collective-permute-start | bytes 1179656 | tf_op jit(solution)/shard_map/ppermute | solution.py:10
  16.7 12.5 %collective-permute-start.1 = (bf16[2,256,384]{2,1,0:T(8,128)(2,1)S(1)}, bf16[2,256,384]{2,1,0:T(8,128)(2,1)S(1)}, u32[]{:S(2)}, u32[]{:S(2)}) collective-permute-start(bf16[2,256,384]{2,1,0:T(8,128)(2,1)S(1)} %get-tuple-element.15), channel_id=1, source_target_pairs={{4,0},{8,4},{12,8},{5,1},{9,5},{13,9},{6,2},{10,6},{14,10},{7,3},{... | collective-permute-start | bytes 1179656 | tf_op jit(solution)/shard_map/ppermute | solution.py:10
  30.5 139.4 %all-reduce.2.cloned.1.call-start = ((), (), s32[]{:S(2)}) async-start(), calls=%async_computation.2 | async-start | bytes 3538944 | tf_op jit(solution)/shard_map/psum | solution.py:66
  47.6 1.6 copy-start.1
  50.1 40.9 %collective-permute-start.2 = (f32[3,384,384]{2,1,0:T(8,128)S(1)}, f32[3,384,384]{2,1,0:T(8,128)S(1)}, u32[]{:S(2)}, u32[]{:S(2)}) collective-permute-start(f32[3,384,384]{2,1,0:T(8,128)S(1)} %fusion.38), channel_id=1, source_target_pairs={{0,2},{2,0},{1,3},{3,1},{4,6},{6,4},{5,7},{7,5},{8,10},{10,8},{9,1... | collective-permute-start | bytes 5308424 | tf_op jit(solution)/shard_map/ppermute | solution.py:62
Sparse Core Ops, SparseCore 0:
  30.6 12.2 all-gather.1
  93.2 76.6 all-reduce.1
where the time goes:
time: 180 us; the launch traced here: 179 us
  waiting for transfers between devices  112 us (62%)
  local copies, waits for them, and re-layouts  21.9 us (12%)
  between operations  14.2 us (8%)
  matrix products  11.3 us (6%)
  starting transfers between devices  8.15 us (5%)
  other arithmetic  6.57 us (4%)
  blocking collectives  5.63 us (3%)
    psum x1, waiting for transfers between devices, shards(): weight_grad = lax.psum(summed, 'seq')  50.3 us
    ppermute x1, waiting for transfers between devices, shards(): summed = keep + lax.ppermute(send, 'batch', [(0, 1), (1, 0)])  39.1 us
    all_gather x1, waiting for transfers between devices, shards(): full_ext = lax.all_gather(own_ext, 'chan', axis=2, tiled=True)  11.2 us
    ppermute x2, waiting for transfers between devices, shift_from(): return lax.ppermute(block, axis, route)  11.2 us
    unnamed x6, local copies, waits for them, and re-layouts  6.76 us
    ppermute x2, starting transfers between devices, shift_from(): return lax.ppermute(block, axis, route)  6.27 us
    all_to_all x1, blocking collectives, shards(): weight_cols = lax.all_to_all(conv_weight, 'chan', 2, 1, tiled=True)  5.63 us
    slice x1, local copies, waits for them, and re-layouts, shards(): cot_full[(2 - k) * spread:(2 - k) * spread + rows]  4.6 us
  transfers between devices with their start and end apart: 5, of which 5 were waited for; matrix products, arithmetic and copies ran while one was open for 12% of the time, Pallas kernels for 0%

commit v1 on v0

--- a/solution.py
+++ b/solution.py
@@ -63,7 +63,8 @@
     else:
         partial = jnp.einsum("tki,to->kio", own_taps, cot_mid, preferred_element_type=jnp.float32)
         summed = lax.psum_scatter(partial, "batch", scatter_dimension=2, tiled=True)
-    weight_grad = lax.psum(summed, "seq")
+    out_arr = lax.all_gather(summed, "seq")
+    weight_grad = jnp.sum(out_arr, 0)
     return (block_out[None], input_grad[None], weight_grad)
 
 

time: 180 us -> 235 us (1.31)
  waiting for transfers between devices: 112 us -> 162 us
  other arithmetic: 6.57 us -> 11.5 us
    all_gather x0 -> x1, waiting for transfers between devices: none -> 101 us  [shards(): out_arr = lax.all_gather(summed, 'seq')]
    psum x1 -> x0, waiting for transfers between devices: 50.3 us -> none  [shards(): weight_grad = lax.psum(summed, 'seq')]
    reduce_sum x0 -> x1, other arithmetic: none -> 4.78 us  [shards(): weight_grad = jnp.sum(out_arr, 0)]
    ppermute x2, waiting for transfers between devices: 11.2 us -> 8.33 us  [shift_from(): return lax.ppermute(block, axis, route)]
    unnamed x6 -> x7, local copies, waits for them, and re-layouts: 6.76 us -> 3.97 us
  transfers between devices with their start and end apart: 5 -> 5, of which waited for: 5 -> 5; matrix products, arithmetic and copies ran while one was open for 12% -> 10% of each run, Pallas kernels for 0% -> 0%
where the time goes in v1:
time: 235 us; the launch traced here: 234 us
  waiting for transfers between devices  162 us (69%)
  local copies, waits for them, and re-layouts  21.9 us (9%)
  between operations  14.2 us (6%)
  other arithmetic  11.5 us (5%)
  matrix products  10.6 us (5%)
  starting transfers between devices  8.78 us (4%)
  blocking collectives  5.63 us (2%)
    all_gather x1, waiting for transfers between devices, shards(): out_arr = lax.all_gather(summed, 'seq')  101 us
    ppermute x1, waiting for transfers between devices, shards(): summed = keep + lax.ppermute(send, 'batch', [(0, 1), (1, 0)])  39.1 us
    all_gather x1, waiting for transfers between devices, shards(): full_ext = lax.all_gather(own_ext, 'chan', axis=2, tiled=True)  13.3 us
    ppermute x2, waiting for transfers between devices, shift_from(): return lax.ppermute(block, axis, route)  8.33 us
    ppermute x2, starting transfers between devices, shift_from(): return lax.ppermute(block, axis, route)  6.9 us
    all_to_all x1, blocking collectives, shards(): weight_cols = lax.all_to_all(conv_weight, 'chan', 2, 1, tiled=True)  5.63 us
    reduce_sum x1, other arithmetic, shards(): weight_grad = jnp.sum(out_arr, 0)  4.78 us
  transfers between devices with their start and end apart: 5, of which 5 were waited for; matrix products, arithmetic and copies ran while one was open for 10% of the time, Pallas kernels for 0%

profile of v1, /device:TPU:0, one launch (start us, length us, event | category | flops | bytes accessed | tf_op | source)
XLA Modules:
  0.0 234.1 jit_solution(6054210757039204400)
XLA Ops:
  7.2 0.0 all-gather.4.cloned.1.call-start
  7.2 2.2 reshape.129
  9.4 0.0 copy-start.1
  9.4 1.9 reduce_sum.18
  11.3 0.3 fusion.27
  11.6 0.0 copy-done.1
  11.6 0.1 fusion.39
  11.7 1.3 collective-permute-start.1
  13.0 5.6 %collective-permute-start = (bf16[2,256,384]{2,1,0:T(8,128)(2,1)S(1)}, bf16[2,256,384]{2,1,0:T(8,128)(2,1)S(1)}, u32[]{:S(2)}, u32[]{:S(2)}) collective-permute-start(bf16[2,256,384]{2,1,0:T(8,128)(2,1)S(1)} %get-tuple-element.14), channel_id=1, source_target_pairs={{0,4},{4,8},{8,12},{1,5},{5,9},{9,13},{2,6},{6,10},{10,14},{3,7},{... | collective-permute-start | bytes 1179656 | tf_op jit(solution)/shard_map/ppermute | solution.py:10
  18.6 7.2 %collective-permute-done.1 = bf16[2,256,384]{2,1,0:T(8,128)(2,1)S(1)} collective-permute-done((bf16[2,256,384]{2,1,0:T(8,128)(2,1)S(1)}, bf16[2,256,384]{2,1,0:T(8,128)(2,1)S(1)}, u32[]{:S(2)}, u32[]{:S(2)}) %collective-permute-start.1) | collective-permute-done | bytes 393248 | tf_op jit(solution)/shard_map/ppermute | solution.py:10
  25.7 1.2 collective-permute-done
  26.9 1.3 pad_maximum_fusion.1
  28.2 0.0 all-gather.4.cloned.1.call-update
  28.2 0.0 all-gather.6.cloned.1.call-start
  28.3 1.0 fusion.35
  29.3 0.1 fusion.41
  29.4 13.3 %all-gather.4.cloned.1.call-done = bf16[2,1024,768]{2,1,0:T(8,128)(2,1)} async-done(((bf16[2,1024,384]{2,1,0:T(8,128)(2,1)}), bf16[2,1024,768]{2,1,0:T(8,128)(2,1)}) %all-gather.4.cloned.1.call-update) | async-done | bytes 3145744 | tf_op jit(solution)/shard_map/all_gather | solution.py:32
  42.8 4.7 %fusion.45 = (bf16[1,512,768]{2,1,0:T(8,128)(2,1)S(1)}, bf16[512,1,768]{2,0,1:T(8,128)(2,1)}, bf16[512,1,768]{2,0,1:T(8,128)(2,1)}, bf16[512,1,768]{2,0,1:T(8,12...) fusion(bf16[2,1024,768]{2,1,0:T(8,128)(2,1)} %all-gather.4.cloned.1.call-done), kind=kLoop, calls=%fused_computation.67 | loop fusion | bytes 10223616 | tf_op jit(solution)/shard_map/slice | solution.py:43
  47.4 0.2 reshape.128
  47.6 0.0 copy-start.2
  47.6 1.6 constant_dynamic-slice_fusion.1
  49.2 0.0 copy-done.2
  49.2 0.8 fusion.38
  50.1 1.8 collective-permute-start.2
  51.9 39.1 %collective-permute-done.2 = f32[3,384,384]{2,1,0:T(8,128)S(1)} collective-permute-done((f32[3,384,384]{2,1,0:T(8,128)S(1)}, f32[3,384,384]{2,1,0:T(8,128)S(1)}, u32[]{:S(2)}, u32[]{:S(2)}) %collective-permute-start.2) | collective-permute-done | bytes 1769504 | tf_op jit(solution)/shard_map/ppermute | solution.py:62
  90.9 2.1 convolution_add_fusion
  93.0 0.0 all-gather.6.cloned.1.call-update
  93.0 4.0 %copy.21 = bf16[3,384,768]{1,0,2:T(4,128)(2,1)S(1)} copy(bf16[3,384,768]{2,1,0:T(8,128)(2,1)} %param.4) | data formatting | bytes 3538944 | tf_op args[1]
  97.0 5.6 %all_to_all.15 = bf16[3,384,768]{1,0,2:T(4,128)(2,1)S(1)} all-to-all(bf16[3,384,768]{1,0,2:T(4,128)(2,1)S(1)} %copy.21), channel_id=1, replica_groups=mesh['group'=2,'seq'=4,'batch'=2,'chan'=2] {'chan'}, dimensions={2} | all-to-all | bytes 3538944 | tf_op jit(solution)/shard_map/all_to_all | solution.py:34
  102.6 0.2 copy.22
  102.8 2.3 copy.23
  105.1 2.1 pad_maximum_fusion
  107.2 2.6 %copy.20 = bf16[512,3,768]{0,2,1:T(8,128)(2,1)} copy(bf16[512,3,768]{2,0,1:T(8,128)(2,1)S(1)} %pad_maximum_fusion) | data formatting | bytes 4718592 | tf_op jit(solution)/shard_map/stack | solution.py:35
  109.7 4.0 %fusion.19 = bf16[512,384]{1,0:T(8,128)(2,1)S(1)} fusion(bf16[3,384,768]{2,1,0:T(8,128)(2,1)} %param.4, bf16[512,1,768]{2,0,1:T(8,128)(2,1)} %get-tuple-element.5, bf16[512,1,768]{2,0,1:T(8,128)(2,1)} %get-tuple-element.4, bf16[512,1,768]{2,0,1:T(8,128)(2,1)} %get-tuple-element.6, f32[512,384]{1,0:T(8,128)S(1)} %reduce_sum.18, ...), kind=kOutput, calls=%fused_computation.26 | convolution fusion | flops 913047552 | bytes 5701632 | tf_op jit(solution)/shard_map/tko,kio->ti/dot_general | solution.py:45
  113.8 0.0 copy-start
  113.8 1.3 broadcast_in_dim.8
  115.1 3.0 %convert_element_type.60 = bf16[1,1024,384]{2,1,0:T(8,128)(2,1)} reshape(bf16[512,2,384]{2,1,0:T(2,128)(2,1)} %broadcast_in_dim.8) | data formatting | bytes 1572864 | tf_op jit(solution)/shard_map/convert_element_type | solution.py:50
  118.0 0.0 copy-done
  118.0 3.7 %fusion.10 = bf16[1,512,384]{2,1,0:T(8,128)(2,1)} fusion(bf16[512,2304]{0,1:T(8,128)(2,1)S(1)} %bitcast.46, bf16[2304,384]{1,0:T(8,128)(2,1)} %bitcast.49, f32[512,384]{1,0:T(8,128)S(1)} %reduce_sum.18), kind=kOutput, calls=%fused_computation.12 | convolution fusion | flops 906559488 | bytes 5308416 | tf_op jit(solution)/shard_map/dot_general | solution.py:36
  121.7 100.8 %all-gather.6.cloned.1.call-done = f32[12,384,384]{2,1,0:T(8,128)} async-done(((f32[3,384,384]{2,1,0:T(8,128)}), f32[12,384,384]{2,1,0:T(8,128)}) %all-gather.6.cloned.1.call-update) | async-done | bytes 7077904 | tf_op jit(solution)/shard_map/all_gather | solution.py:66
  222.5 4.8 %reduce_sum.19 = f32[3,384,384]{2,1,0:T(8,128)} reduce(f32[4,3,384,384]{3,2,1,0:T(8,128)} %bitcast.47, f32[]{:T(128)} %constant.8.clone.1), dimensions={0}, to_apply=%region_1.2 | reduce | flops 1327104 | bytes 8847364 | tf_op jit(solution)/shard_map/reduce_sum | solution.py:67
Async XLA Ops:
  7.2 35.6 %all-gather.4.cloned.1.call-start = ((), (), s32[]{:S(2)}) async-start(), calls=%async_computation.1 | async-start | bytes 4718592 | tf_op jit(solution)/shard_map/all_gather | solution.py:32
  9.4 2.2 copy-start.1
  11.7 14.1 %collective-permute-start.1 = (bf16[2,256,384]{2,1,0:T(8,128)(2,1)S(1)}, bf16[2,256,384]{2,1,0:T(8,128)(2,1)S(1)}, u32[]{:S(2)}, u32[]{:S(2)}) collective-permute-start(bf16[2,256,384]{2,1,0:T(8,128)(2,1)S(1)} %get-tuple-element.15), channel_id=1, source_target_pairs={{4,0},{8,4},{12,8},{5,1},{9,5},{13,9},{6,2},{10,6},{14,10},{7,3},{... | collective-permute-start | bytes 1179656 | tf_op jit(solution)/shard_map/ppermute | solution.py:10
  13.0 13.9 %collective-permute-start = (bf16[2,256,384]{2,1,0:T(8,128)(2,1)S(1)}, bf16[2,256,384]{2,1,0:T(8,128)(2,1)S(1)}, u32[]{:S(2)}, u32[]{:S(2)}) collective-permute-start(bf16[2,256,384]{2,1,0:T(8,128)(2,1)S(1)} %get-tuple-element.14), channel_id=1, source_target_pairs={{0,4},{4,8},{8,12},{1,5},{5,9},{9,13},{2,6},{6,10},{10,14},{3,7},{... | collective-permute-start | bytes 1179656 | tf_op jit(solution)/shard_map/ppermute | solution.py:10
  28.2 194.3 %all-gather.6.cloned.1.call-start = ((), (), s32[]{:S(2)}) async-start(), calls=%async_computation.2 | async-start | bytes 8847360 | tf_op jit(solution)/shard_map/all_gather | solution.py:66
  47.6 1.6 copy-start.2
  50.1 40.9 %collective-permute-start.2 = (f32[3,384,384]{2,1,0:T(8,128)S(1)}, f32[3,384,384]{2,1,0:T(8,128)S(1)}, u32[]{:S(2)}, u32[]{:S(2)}) collective-permute-start(f32[3,384,384]{2,1,0:T(8,128)S(1)} %fusion.38), channel_id=1, source_target_pairs={{0,2},{2,0},{1,3},{3,1},{4,6},{6,4},{5,7},{7,5},{8,10},{10,8},{9,1... | collective-permute-start | bytes 5308424 | tf_op jit(solution)/shard_map/ppermute | solution.py:62
  113.8 4.2 %copy-start = (bf16[512,3,768]{0,2,1:T(8,128)(2,1)S(1)}, bf16[512,3,768]{0,2,1:T(8,128)(2,1)}, u32[]{:S(2)}) copy-start(bf16[512,3,768]{0,2,1:T(8,128)(2,1)} %copy.20) | copy-start | bytes 7077892
Sparse Core Ops, SparseCore 0:
  28.4 14.3 all-gather.3
  93.1 129.3 all-gather.5
